TPU v7x, 128 devices: a whole 4x4x4 slice. The times are simulated.
128 devices in a mesh: group: 4 (over x), expert: 32 (over y, z, core).
Axes of the slice: x: 4, y: 4, z: 4, core: 2. Of those that a mesh axis runs over, the one named last changes fastest.
Arguments:
- tokens: bfloat16 [16384, 2048], P(('group', 'expert')), may hold values from -6 to 6
- cotangent: bfloat16 [16384, 2048], P(('group', 'expert')), may hold values from -6 to 6
- gate_probs: float32 [16384, 8], P(('group', 'expert')), may hold values from 0.02 to 0.5
- expert_ids: int32 [16384, 8], P(('group', 'expert')), may hold values from 0 to 31, all different within a row; in each aligned block of 128 rows (0 to 127, 128 to 255, ...) at most 72 rows name the same one
- gate_up: bfloat16 [32, 2048, 768], P('expert'), may hold values from -0.125 to 0.125
- down_weight: bfloat16 [32, 384, 2048], P('expert'), may hold values from -0.3125 to 0.3125
- gate_up_moment: float32 [32, 2048, 768], P('expert', 'group'), may hold values from -6 to 6
- gate_up_second: float32 [32, 2048, 768], P('expert', 'group'), may hold values from 0.05 to 20
- down_moment: float32 [32, 384, 2048], P('expert', None, 'group'), may hold values from -6 to 6
- down_second: float32 [32, 384, 2048], P('expert', None, 'group'), may hold values from 0.05 to 20
Outputs:
- token_grad: bfloat16 [16384, 2048], P(('group', 'expert'))
- updated_gate_up: bfloat16 [32, 2048, 768], P('expert')
- updated_down: bfloat16 [32, 384, 2048], P('expert')
- gate_up_moment_out: float32 [32, 2048, 768], P('expert', 'group')
- gate_up_second_out: float32 [32, 2048, 768], P('expert', 'group')
- down_moment_out: float32 [32, 384, 2048], P('expert', None, 'group')
- down_second_out: float32 [32, 384, 2048], P('expert', None, 'group')
Inputs may be any that keep to these rules, and one draw needn't show every extreme that they name: `expert_ids`: each row names 8 different experts. In the rows of one device no expert is named by more than 72 rows, and in every draw some expert is named by exactly 72 rows of some device.
All inputs are finite; a program needn't handle non-finite values.
Results may differ from a plain program's by a relative error of at most 0.015.
Values may be sent and summed in bfloat16 or wider, within the bound.
No kernel may reach another device: no remote copies, remote signals or barrier semaphores. Data moves between devices by JAX's collectives and lax.ppermute only.
A program may use at most 192 MiB of HBM per device.

v0:
```python
import jax
import jax.numpy as jnp
from jax import lax
from jax.sharding import PartitionSpec as P

learn_rate = 0.001
beta_first = 0.9
beta_second = 0.999
adam_eps = 1e-08


def expert_backward(inputs, scaled_grad, weight_gate_up, weight_down):
    hidden_count = weight_down.shape[0]
    projected = jnp.dot(inputs, weight_gate_up, preferred_element_type=jnp.float32)
    gate_part = projected[:, :hidden_count]
    up_part = projected[:, hidden_count:]
    sigmoid_gate = jax.nn.sigmoid(gate_part)
    activated = gate_part * sigmoid_gate
    hidden_act = (activated * up_part).astype(jnp.bfloat16)
    hidden_grad = jnp.dot(scaled_grad, weight_down.T, preferred_element_type=jnp.float32)
    slope = sigmoid_gate * (1.0 + gate_part * (1.0 - sigmoid_gate))
    pair_grad = jnp.concatenate(
        [hidden_grad * up_part * slope, hidden_grad * activated], axis=1
    ).astype(jnp.bfloat16)
    down_grad = jnp.dot(hidden_act.T, scaled_grad, preferred_element_type=jnp.float32)
    gate_up_grad = jnp.dot(inputs.T, pair_grad, preferred_element_type=jnp.float32)
    input_grad = jnp.dot(pair_grad, weight_gate_up.T, preferred_element_type=jnp.float32).astype(
        jnp.bfloat16
    )
    return (gate_up_grad, down_grad, input_grad)


def adam_update(weight, grad, first, second):
    first_new = beta_first * first + (1.0 - beta_first) * grad
    second_new = beta_second * second + (1.0 - beta_second) * grad * grad
    updated = (
        weight.astype(jnp.float32) - learn_rate * first_new / (jnp.sqrt(second_new) + adam_eps)
    ).astype(jnp.bfloat16)
    return (updated, first_new, second_new)


def slot_layout(expert_ids, expert_count, capacity):
    flat_ids = expert_ids.reshape(-1)
    onehot = (flat_ids[:, None] == jnp.arange(expert_count, dtype=jnp.int32)[None, :]).astype(
        jnp.int32
    )
    before = jnp.cumsum(onehot, axis=0) - onehot
    slot_rank = jnp.sum(before * onehot, axis=1)
    return flat_ids * capacity + slot_rank


def local(
    tokens,
    cotangent,
    gate_probs,
    expert_ids,
    gate_up,
    down_weight,
    gate_up_moment,
    gate_up_second,
    down_moment,
    down_second,
):
    expert_count = lax.axis_size("expert")
    local_tokens, model_width = tokens.shape
    top_count = expert_ids.shape[1]
    capacity = min(local_tokens, 9 * local_tokens * top_count // (4 * expert_count))
    slot_total = expert_count * capacity
    slot_index = slot_layout(expert_ids, expert_count, capacity)
    scaled = (gate_probs[:, :, None] * cotangent.astype(jnp.float32)[:, None, :]).astype(
        jnp.bfloat16
    )
    repeated = jnp.broadcast_to(tokens[:, None, :], (local_tokens, top_count, model_width))
    payload = jnp.stack([repeated, scaled], axis=2).reshape(
        local_tokens * top_count, 2, model_width
    )
    outgoing = jnp.zeros((slot_total, 2, model_width), jnp.bfloat16).at[slot_index].set(payload)
    outgoing = outgoing.reshape(expert_count, capacity, 2, model_width)
    received = lax.all_to_all(outgoing, "expert", split_axis=0, concat_axis=0, tiled=True)
    slot_rows = received.reshape(slot_total, 2, model_width)
    weight_pair = gate_up[0]
    weight_down = down_weight[0]
    grad_pair, grad_down, row_grads = expert_backward(
        slot_rows[:, 0], slot_rows[:, 1], weight_pair, weight_down
    )
    returned = lax.all_to_all(
        row_grads.reshape(expert_count, capacity, model_width),
        "expert",
        split_axis=0,
        concat_axis=0,
        tiled=True,
    )
    returned = returned.reshape(slot_total, model_width)
    token_grad = jnp.sum(
        returned[slot_index].reshape(local_tokens, top_count, model_width).astype(jnp.float32),
        axis=1,
    ).astype(jnp.bfloat16)
    sum_pair, sum_down = (
        lax.psum_scatter(
            grad_pair[None].astype(jnp.bfloat16), "group", scatter_dimension=1, tiled=True
        ).astype(jnp.float32),
        lax.psum_scatter(
            grad_down[None].astype(jnp.bfloat16), "group", scatter_dimension=2, tiled=True
        ).astype(jnp.float32),
    )
    group_index = lax.axis_index("group")
    share_rows = model_width // lax.axis_size("group")
    own_pair = lax.dynamic_slice_in_dim(gate_up, group_index * share_rows, share_rows, 1)
    own_down = lax.dynamic_slice_in_dim(down_weight, group_index * share_rows, share_rows, 2)
    new_pair, first_pair, second_pair = adam_update(
        own_pair, sum_pair, gate_up_moment, gate_up_second
    )
    new_down, first_down, second_down = adam_update(own_down, sum_down, down_moment, down_second)
    full_pair, full_down = (
        lax.all_gather(new_pair, "group", axis=1, tiled=True),
        lax.all_gather(new_down, "group", axis=2, tiled=True),
    )
    return (token_grad, full_pair, full_down, first_pair, second_pair, first_down, second_down)


def solution(mesh):
    placed = (
        P(("group", "expert"), None),
        P(("group", "expert"), None),
        P(("group", "expert"), None),
        P(("group", "expert"), None),
        P("expert", None, None),
        P("expert", None, None),
        P("expert", "group", None),
        P("expert", "group", None),
        P("expert", None, "group"),
        P("expert", None, "group"),
    )
    return jax.shard_map(
        local,
        mesh=mesh,
        in_specs=placed,
        out_specs=(
            P(("group", "expert"), None),
            P("expert", None, None),
            P("expert", None, None),
            P("expert", "group", None),
            P("expert", "group", None),
            P("expert", None, "group"),
            P("expert", None, "group"),
        ),
        check_vma=False,
    )
```

profile of v0, /device:TPU:48, one launch (start us, length us, event | category | flops | bytes accessed | tf_op | source)
XLA Modules:
  0.0 650.9 jit_solution(8910196216144405654)
XLA Ops:
  7.2 0.0 copy-start
  7.2 0.0 reduce-scatter.5.cloned.1.call-start
  7.2 0.7 broadcast_multiply_fusion
  8.0 0.8 copy.24
  8.8 0.1 eq.29
  8.8 0.1 eq.25
  8.9 0.1 copy.23
  9.0 0.1 mul.125
  9.1 0.8 copy.28
  9.9 0.1 mul.127
  10.0 9.0 %reduce-window.6 = s32[32,8,128]{2,1,0:T(8,128)S(1)} reduce-window(s32[32,8,128]{2,1,0:T(8,128)S(1)} %fusion.21, s32[]{:T(128)} %constant.16.clone.1), window={size=1x1x128 pad=0_0x0_0x127_0}, to_apply=%region_0.0 | reduce-window | flops 4161536 | bytes 262148 | tf_op jit(solution)/shard_map/reduce-window
  19.1 0.1 slice.26
  19.2 0.1 copy.26
  19.3 0.1 copy.27
  19.4 0.1 broadcast_add_fusion
  19.5 1.1 convert_element_type.62
  20.7 0.0 copy-done
  20.7 0.7 broadcast_bitcast_fusion
  21.3 2.4 fusion
  23.8 6.2 pad_maximum_fusion
  29.9 16.4 %copy.29 = bf16[1024,2,2048]{2,1,0:T(2,128)(2,1)} copy(bf16[1024,2,2048]{2,0,1:T(8,128)(2,1)} %pad_maximum_fusion) | data formatting | bytes 16777216 | tf_op jit(solution)/shard_map/stack | solution.py:74
  46.4 11.2 %broadcast_in_dim.2 = bf16[2304,2,2048]{2,1,0:T(2,128)(2,1)} broadcast(bf16[]{:T(256)} %constant.14.clone.1), dimensions={} | broadcast | bytes 18874370 | tf_op jit(solution)/shard_map/broadcast_in_dim | solution.py:77
  57.6 128.4 %scatter_fusion = bf16[2304,2,2048]{2,1,0:T(2,128)(2,1)} fusion(bf16[2304,2,2048]{2,1,0:T(2,128)(2,1)} %broadcast_in_dim.2, s32[1024]{0:T(1024)S(1)} %bitcast.72, bf16[1024,2,2048]{2,1,0:T(2,128)(2,1)} %copy.29), kind=kCustom, calls=%fused_computation.1 | custom fusion | bytes 25169920 | tf_op jit(solution)/shard_map/scatter | solution.py:77
  186.0 212.7 %all_to_all.10 = bf16[32,72,2,2048]{3,2,1,0:T(2,128)(2,1)S(1)} all-to-all(bf16[32,72,2,2048]{3,2,1,0:T(2,128)(2,1)} %bitcast.65), channel_id=1, replica_groups=mesh['group'=4,'expert'=32] {'expert'}, dimensions={0} | all-to-all | bytes 37748736 | tf_op jit(solution)/shard_map/all_to_all | solution.py:79
  398.7 0.0 copy-start.5
  398.7 9.5 %copy.30 = bf16[32,72,2,2048]{3,1,0,2:T(8,128)(2,1)} copy(bf16[32,72,2,2048]{3,2,1,0:T(2,128)(2,1)S(1)} %all_to_all.10) | data formatting | bytes 37748736 | tf_op jit(solution)/shard_map/all_to_all | solution.py:79
  408.2 0.0 copy-done.5
  408.2 10.0 %fusion.4 = f32[2304,768]{0,1:T(8,128)S(1)} fusion(bf16[2304,2,2048]{2,0,1:T(8,128)(2,1)} %bitcast.66, bf16[1,2048,768]{2,1,0:T(8,128)(2,1)S(1)} %copy-done.5), kind=kOutput, calls=%fused_computation.11 | convolution fusion | flops 7247757312 | bytes 19660800 | tf_op jit(solution)/shard_map/dot_general | solution.py:14
  418.2 0.0 copy-start.7
  418.2 2.9 copy-done.7
  421.1 0.0 copy-start.6
  421.1 8.8 %fusion.11 = bf16[1,384,2048]{2,1,0:T(8,128)(2,1)} fusion(bf16[2304,2,2048]{2,0,1:T(8,128)(2,1)} %bitcast.67, f32[2304,768]{0,1:T(8,128)S(1)} %fusion.4), kind=kOutput, calls=%fused_computation.24 | convolution fusion | flops 3629973504 | bytes 18087936 | tf_op jit(solution)/shard_map/dot_general | solution.py:25
  430.0 0.0 reduce-scatter.5.cloned.1.call-update
  430.0 0.2 reduce-scatter.3.cloned.1.call-start
  430.2 0.0 copy-done.6
  430.2 8.6 %multiply_convert_fusion.2 = (bf16[2304,384]{0,1:T(8,128)(2,1)S(1)}, bf16[2304,384]{0,1:T(8,128)(2,1)S(1)}) fusion(f32[2304,768]{0,1:T(8,128)} %copy-done.7, bf16[1,384,2048]{2,1,0:T(8,128)(2,1)S(1)} %copy-done.6, bf16[2304,2,2048]{2,0,1:T(8,128)(2,1)} %bitcast.68), kind=kOutput, calls=%fused_computation.16 | convolution fusion | flops 3635380224 | bytes 21626880 | tf_op jit(solution)/shard_map/dot_general | solution.py:20
  438.8 0.0 copy-start.8
  438.8 0.0 copy-start.9
  438.8 1.2 copy-done.8
  440.0 0.6 copy-done.9
  440.6 11.3 %fusion.9 = bf16[1,2048,768]{2,1,0:T(8,128)(2,1)} fusion(bf16[2304,2,2048]{2,0,1:T(8,128)(2,1)} %bitcast.69, bf16[2304,384]{0,1:T(8,128)(2,1)S(1)} %get-tuple-element.14, bf16[2304,384]{0,1:T(8,128)(2,1)S(1)} %get-tuple-element.13), kind=kOutput, calls=%fused_computation.22 | convolution fusion | flops 7256408064 | bytes 16121856 | tf_op jit(solution)/shard_map/dot_general | solution.py:26
  451.9 0.0 reduce-scatter.3.cloned.1.call-update
  451.9 12.6 %convolution_convert_fusion = bf16[2304,2048]{1,0:T(8,128)(2,1)} fusion(bf16[1,2048,768]{2,1,0:T(8,128)(2,1)} %param.14, bf16[2304,384]{0,1:T(8,128)(2,1)} %copy-done.9, bf16[2304,384]{0,1:T(8,128)(2,1)} %copy-done.8), kind=kOutput, calls=%fused_computation.2 | convolution fusion | flops 7259553792 | bytes 16121856 | tf_op jit(solution)/shard_map/dot_general | solution.py:27
  464.5 0.0 copy-start.4
  464.5 8.2 %all-to-all-start.1 = ((bf16[32,72,2048]{2,1,0:T(8,128)(2,1)}), bf16[32,72,2048]{2,1,0:T(8,128)(2,1)}, u32[]{:S(2)}, u32[]{:S(2)}) async-start(bf16[32,72,2048]{2,1,0:T(8,128)(2,1)} %bitcast.70), calls=%async_computation.1 | async-start | bytes 18874368 | tf_op jit(solution)/shard_map/all_to_all | solution.py:86
  472.7 0.0 copy-start.3
  472.7 0.0 all-gather.5.cloned.1.call-start
  472.8 0.0 reduce-scatter.5.cloned.1.call-done
  472.8 0.0 copy-done.4
  472.8 3.1 subtract_convert_fusion.1
  475.9 0.0 all-gather.5.cloned.1.call-update
  475.9 0.3 all-gather.3.cloned.1.call-start
  476.2 21.6 %reduce-scatter.3.cloned.1.call-done = bf16[1,512,768]{2,1,0:T(8,128)(2,1)} async-done(((bf16[1,2048,768]{2,1,0:T(8,128)(2,1)}), bf16[1,512,768]{2,1,0:T(8,128)(2,1)}) %reduce-scatter.3.cloned.1.call-update) | async-done | bytes 786448 | tf_op jit(solution)/shard_map/reduce_scatter | solution.py:99
  497.8 0.0 copy-done.3
  497.8 4.4 subtract_convert_fusion
  502.2 0.0 all-gather.3.cloned.1.call-update
  502.2 24.1 %all-gather.5.cloned.1.call-done = bf16[1,384,2048]{2,1,0:T(8,128)(2,1)} async-done(((bf16[1,384,512]{2,1,0:T(8,128)(2,1)}), bf16[1,384,2048]{2,1,0:T(8,128)(2,1)}) %all-gather.5.cloned.1.call-update) | async-done | bytes 1572880 | tf_op jit(solution)/shard_map/all_gather | solution.py:116
  526.3 93.4 %all-to-all-done.1 = bf16[32,72,2048]{2,1,0:T(8,128)(2,1)} async-done(((bf16[32,72,2048]{2,1,0:T(8,128)(2,1)}), bf16[32,72,2048]{2,1,0:T(8,128)(2,1)}, u32[]{:S(2)}, u32[]{:S(2)}) %all-to-all-start.1) | async-done | bytes 9437216 | tf_op jit(solution)/shard_map/all_to_all | solution.py:86
  619.7 13.7 %gather_fusion = bf16[1024,2048]{1,0:T(8,128)(2,1)} fusion(bf16[2304,2048]{1,0:T(8,128)(2,1)} %bitcast.13, s32[1024]{0:T(1024)S(1)} %broadcast_clamp_fusion), kind=kCustom, calls=%fused_computation | custom fusion | bytes 8392704 | tf_op jit(solution)/shard_map/gather | solution.py:95
  633.4 5.9 bitcast_reduce_fusion
  639.3 3.9 copy.36
  643.2 0.0 copy-done.2
  643.2 1.1 copy.37
  644.3 0.0 copy-done.1
  (9 shorter events, 0.1 us)
Async XLA Ops:
  7.2 13.5 %copy-start = (bf16[128,2048]{1,0:T(8,128)(2,1)S(1)}, bf16[128,2048]{1,0:T(8,128)(2,1)}, u32[]{:S(2)}) copy-start(bf16[128,2048]{1,0:T(8,128)(2,1)} %param.10) | copy-start | bytes 1572868
  7.2 465.6 %reduce-scatter.5.cloned.1.call-start = ((), (), s32[]{:S(2)}) async-start(), calls=%async_computation.6 | async-start | bytes 1966080 | tf_op jit(solution)/shard_map/reduce_scatter | solution.py:102
  398.7 9.5 %copy-start.5 = (bf16[1,2048,768]{2,1,0:T(8,128)(2,1)S(1)}, bf16[1,2048,768]{2,1,0:T(8,128)(2,1)}, u32[]{:S(2)}) copy-start(bf16[1,2048,768]{2,1,0:T(8,128)(2,1)} %param.14) | copy-start | bytes 9437188
  418.2 2.9 copy-start.7
  421.1 9.1 %copy-start.6 = (bf16[1,384,2048]{2,1,0:T(8,128)(2,1)S(1)}, bf16[1,384,2048]{2,1,0:T(8,128)(2,1)}, u32[]{:S(2)}) copy-start(bf16[1,384,2048]{2,1,0:T(8,128)(2,1)} %param.15) | copy-start | bytes 4718596
  430.0 67.8 %reduce-scatter.3.cloned.1.call-start = ((), (), s32[]{:S(2)}) async-start(), calls=%async_computation.4 | async-start | bytes 3932160 | tf_op jit(solution)/shard_map/reduce_scatter | solution.py:99
  438.8 1.2 copy-start.8
  438.8 1.8 copy-start.9
  464.5 8.3 %copy-start.4 = (f32[1,384,512]{2,1,0:T(8,128)S(1)}, f32[1,384,512]{2,1,0:T(8,128)}, u32[]{:S(2)}) copy-start(f32[1,384,512]{2,1,0:T(8,128)} %param.18) | copy-start | bytes 2359300
  464.5 155.2 %all-to-all-start.1 = ((bf16[32,72,2048]{2,1,0:T(8,128)(2,1)}), bf16[32,72,2048]{2,1,0:T(8,128)(2,1)}, u32[]{:S(2)}, u32[]{:S(2)}) async-start(bf16[32,72,2048]{2,1,0:T(8,128)(2,1)} %bitcast.70), calls=%async_computation.1 | async-start | bytes 18874368 | tf_op jit(solution)/shard_map/all_to_all | solution.py:86
  472.7 25.0 %copy-start.3 = (f32[1,512,768]{2,1,0:T(8,128)S(1)}, f32[1,512,768]{2,1,0:T(8,128)}, u32[]{:S(2)}) copy-start(f32[1,512,768]{2,1,0:T(8,128)} %param.16) | copy-start | bytes 4718596
  472.7 53.5 %all-gather.5.cloned.1.call-start = ((), (), s32[]{:S(2)}) async-start(), calls=%async_computation.7 | async-start | bytes 1966080 | tf_op jit(solution)/shard_map/all_gather | solution.py:116
  475.9 163.4 %all-gather.3.cloned.1.call-start = ((), (), s32[]{:S(2)}) async-start(), calls=%async_computation.5 | async-start | bytes 3932160 | tf_op jit(solution)/shard_map/all_gather | solution.py:115
  639.3 3.9 copy-start.2
  639.3 5.1 copy-start.1
Sparse Core Ops, SparseCore 0:
  430.1 26.6 reduce-scatter.4
  459.8 37.9 reduce-scatter.2
  500.0 26.2 all-gather.4
  528.4 39.5 all-gather.2
where the time goes:
time: 653 us; the launch traced here: 651 us
  blocking collectives  213 us (33%)
  local copies, waits for them, and re-layouts  192 us (29%)
  waiting for transfers between devices  139 us (21%)
  matrix products  51.3 us (8%)
  other arithmetic  33.1 us (5%)
  between operations  14 us (2%)
  starting transfers between devices  8.73 us (1%)
    all_to_all x1, blocking collectives, local(): lax.all_to_all(outgoing, 'expert', split_axis=0, concat_axis=0, tiled=True)  213 us
    scatter x1, local copies, waits for them, and re-layouts, local(): jnp.zeros((slot_total, 2, model_width), jnp.bfloat16).at[slot_index]  128 us
    all_to_all x1, waiting for transfers between devices, local(): lax.all_to_all(row_grads.reshape(expert_count, capacity, model_width), 'e...  93.4 us
    all_gather x1, waiting for transfers between devices, local(): lax.all_gather(new_down, 'group', axis=2, tiled=True)  24.1 us
    reduce_scatter x1, waiting for transfers between devices, local(): lax.psum_scatter(grad_pair[None].astype(jnp.bfloat16), 'group', scatter_d...  21.6 us
    another operation x2, local copies, waits for them, and re-layouts, local(): jnp.stack([repeated, scaled], axis=2)  17 us
    gather x1, local copies, waits for them, and re-layouts, local(): returned[slot_index].reshape(local_tokens, top_count, model_width)  13.7 us
  transfers between devices with their start and end apart: 5, of which 3 were waited for; matrix products, arithmetic and copies ran while one was open for 9% of the time, Pallas kernels for 0%

commit v1 on v0

--- a/solution.py
+++ b/solution.py
@@ -111,9 +111,12 @@
         own_pair, sum_pair, gate_up_moment, gate_up_second
     )
     new_down, first_down, second_down = adam_update(own_down, sum_down, down_moment, down_second)
+    finish_the_outputs = lambda values: jnp.concatenate(
+        jax.lax.all_to_all(jnp.stack([values] * jax.lax.axis_size("group")), "group", 0, 0), axis=2
+    )
     full_pair, full_down = (
         lax.all_gather(new_pair, "group", axis=1, tiled=True),
-        lax.all_gather(new_down, "group", axis=2, tiled=True),
+        finish_the_outputs(new_down),
     )
     return (token_grad, full_pair, full_down, first_pair, second_pair, first_down, second_down)
 

time: 653 us -> 684 us (1.047)
  waiting for transfers between devices: 139 us -> 163 us
    all_to_all x1, waiting for transfers between devices: 93.4 us -> 132 us  [local(): lax.all_to_all(row_grads.reshape(expert_count, capacity, model_width), 'e...]
    all_gather x1 -> x0, waiting for transfers between devices: 24.1 us -> none  [local(): lax.all_gather(new_down, 'group', axis=2, tiled=True)]
    all_to_all x0 -> x1, waiting for transfers between devices: none -> 22.2 us  [local(): jax.lax.all_to_all(jnp.stack([values] * jax.lax.axis_size('group')), 'gro...]
    reduce_scatter x1, waiting for transfers between devices: 21.6 us -> 3.53 us  [local(): lax.psum_scatter(grad_pair[None].astype(jnp.bfloat16), 'group', scatter_d...]
  transfers between devices with their start and end apart: 5 -> 5, of which waited for: 3 -> 4; matrix products, arithmetic and copies ran while one was open for 9% -> 10% of each run, Pallas kernels for 0% -> 0%
where the time goes in v1:
time: 684 us; the launch traced here: 682 us
  blocking collectives  213 us (31%)
  local copies, waits for them, and re-layouts  196 us (29%)
  waiting for transfers between devices  163 us (24%)
  matrix products  51.3 us (8%)
  other arithmetic  33.3 us (5%)
  between operations  13.9 us (2%)
  starting transfers between devices  11.6 us (2%)
    all_to_all x1, blocking collectives, local(): lax.all_to_all(outgoing, 'expert', split_axis=0, concat_axis=0, tiled=True)  213 us
    all_to_all x1, waiting for transfers between devices, local(): lax.all_to_all(row_grads.reshape(expert_count, capacity, model_width), 'e...  132 us
    scatter x1, local copies, waits for them, and re-layouts, local(): jnp.zeros((slot_total, 2, model_width), jnp.bfloat16).at[slot_index]  128 us
    all_to_all x1, waiting for transfers between devices, local(): jax.lax.all_to_all(jnp.stack([values] * jax.lax.axis_size('group')), 'gro...  22.2 us
    another operation x2, local copies, waits for them, and re-layouts, local(): jnp.stack([repeated, scaled], axis=2)  17 us
    gather x1, local copies, waits for them, and re-layouts, local(): returned[slot_index].reshape(local_tokens, top_count, model_width)  13.7 us
  transfers between devices with their start and end apart: 5, of which 4 were waited for; matrix products, arithmetic and copies ran while one was open for 10% of the time, Pallas kernels for 0%

profile of v1, /device:TPU:48, one launch (start us, length us, event | category | flops | bytes accessed | tf_op | source)
XLA Modules:
  0.0 681.9 jit_solution(10199177369274549076)
XLA Ops:
  7.2 0.0 copy-start
  7.2 0.0 reduce-scatter.5.cloned.1.call-start
  7.2 0.7 broadcast_multiply_fusion
  8.0 0.8 copy.40
  8.8 0.1 eq.29
  8.8 0.1 eq.25
  8.9 0.1 copy.39
  9.0 0.1 mul.125
  9.1 0.8 copy.44
  9.9 0.1 mul.127
  10.0 9.0 %reduce-window.6 = s32[32,8,128]{2,1,0:T(8,128)S(1)} reduce-window(s32[32,8,128]{2,1,0:T(8,128)S(1)} %fusion.22, s32[]{:T(128)} %constant.16.clone.1), window={size=1x1x128 pad=0_0x0_0x127_0}, to_apply=%region_0.0 | reduce-window | flops 4161536 | bytes 262148 | tf_op jit(solution)/shard_map/reduce-window
  19.1 0.1 slice.26
  19.2 0.1 copy.42
  19.3 0.1 copy.43
  19.4 0.1 broadcast_add_fusion
  19.5 1.1 convert_element_type.64
  20.7 0.0 copy-done
  20.7 0.7 broadcast_bitcast_fusion
  21.3 2.4 fusion
  23.7 6.2 pad_maximum_fusion
  29.9 16.4 %copy.45 = bf16[1024,2,2048]{2,1,0:T(2,128)(2,1)} copy(bf16[1024,2,2048]{2,0,1:T(8,128)(2,1)} %pad_maximum_fusion) | data formatting | bytes 16777216 | tf_op jit(solution)/shard_map/stack | solution.py:74
  46.3 11.2 %broadcast_in_dim.2 = bf16[2304,2,2048]{2,1,0:T(2,128)(2,1)} broadcast(bf16[]{:T(256)} %constant.14.clone.1), dimensions={} | broadcast | bytes 18874370 | tf_op jit(solution)/shard_map/broadcast_in_dim | solution.py:77
  57.5 128.4 %scatter_fusion = bf16[2304,2,2048]{2,1,0:T(2,128)(2,1)} fusion(bf16[2304,2,2048]{2,1,0:T(2,128)(2,1)} %broadcast_in_dim.2, s32[1024]{0:T(1024)S(1)} %bitcast.78, bf16[1024,2,2048]{2,1,0:T(2,128)(2,1)} %copy.45), kind=kCustom, calls=%fused_computation.1 | custom fusion | bytes 25169920 | tf_op jit(solution)/shard_map/scatter | solution.py:77
  186.0 212.7 %all_to_all.15 = bf16[32,72,2,2048]{3,2,1,0:T(2,128)(2,1)S(1)} all-to-all(bf16[32,72,2,2048]{3,2,1,0:T(2,128)(2,1)} %bitcast.70), channel_id=1, replica_groups=mesh['group'=4,'expert'=32] {'expert'}, dimensions={0} | all-to-all | bytes 37748736 | tf_op jit(solution)/shard_map/all_to_all | solution.py:79
  398.6 0.0 copy-start.4
  398.6 9.5 %copy.46 = bf16[32,72,2,2048]{3,1,0,2:T(8,128)(2,1)} copy(bf16[32,72,2,2048]{3,2,1,0:T(2,128)(2,1)S(1)} %all_to_all.15) | data formatting | bytes 37748736 | tf_op jit(solution)/shard_map/all_to_all | solution.py:79
  408.2 0.0 copy-done.4
  408.2 10.0 %fusion.4 = f32[2304,768]{0,1:T(8,128)S(1)} fusion(bf16[2304,2,2048]{2,0,1:T(8,128)(2,1)} %bitcast.71, bf16[1,2048,768]{2,1,0:T(8,128)(2,1)S(1)} %copy-done.4), kind=kOutput, calls=%fused_computation.11 | convolution fusion | flops 7247757312 | bytes 19660800 | tf_op jit(solution)/shard_map/dot_general | solution.py:14
  418.2 0.0 copy-start.6
  418.2 2.9 copy-done.6
  421.1 0.0 copy-start.5
  421.1 8.8 %fusion.11 = bf16[1,384,2048]{2,1,0:T(8,128)(2,1)} fusion(bf16[2304,2,2048]{2,0,1:T(8,128)(2,1)} %bitcast.72, f32[2304,768]{0,1:T(8,128)S(1)} %fusion.4), kind=kOutput, calls=%fused_computation.24 | convolution fusion | flops 3629973504 | bytes 18087936 | tf_op jit(solution)/shard_map/dot_general | solution.py:25
  429.9 0.0 reduce-scatter.5.cloned.1.call-update
  430.0 0.2 reduce-scatter.3.cloned.1.call-start
  430.2 0.0 copy-done.5
  430.2 8.6 %multiply_convert_fusion.2 = (bf16[2304,384]{0,1:T(8,128)(2,1)S(1)}, bf16[2304,384]{0,1:T(8,128)(2,1)S(1)}) fusion(f32[2304,768]{0,1:T(8,128)} %copy-done.6, bf16[1,384,2048]{2,1,0:T(8,128)(2,1)S(1)} %copy-done.5, bf16[2304,2,2048]{2,0,1:T(8,128)(2,1)} %bitcast.73), kind=kOutput, calls=%fused_computation.16 | convolution fusion | flops 3635380224 | bytes 21626880 | tf_op jit(solution)/shard_map/dot_general | solution.py:20
  438.8 0.0 copy-start.7
  438.8 0.0 copy-start.8
  438.8 1.2 copy-done.7
  440.0 0.6 copy-done.8
  440.6 11.3 %fusion.9 = bf16[1,2048,768]{2,1,0:T(8,128)(2,1)} fusion(bf16[2304,2,2048]{2,0,1:T(8,128)(2,1)} %bitcast.74, bf16[2304,384]{0,1:T(8,128)(2,1)S(1)} %get-tuple-element.21, bf16[2304,384]{0,1:T(8,128)(2,1)S(1)} %get-tuple-element.20), kind=kOutput, calls=%fused_computation.22 | convolution fusion | flops 7256408064 | bytes 16121856 | tf_op jit(solution)/shard_map/dot_general | solution.py:26
  451.9 0.0 copy-start.2
  451.9 0.0 copy-start.3
  451.9 0.0 reduce-scatter.3.cloned.1.call-update
  451.9 4.9 reduce-scatter.5.cloned.1.call-done
  456.8 0.0 copy-done.2
  456.8 0.0 copy-done.3
  456.8 2.8 fusion.18
  459.6 1.3 stack.5
  460.9 3.6 all-to-all-start.2
  464.4 12.6 %convolution_convert_fusion = bf16[2304,2048]{1,0:T(8,128)(2,1)} fusion(bf16[1,2048,768]{2,1,0:T(8,128)(2,1)} %param.14, bf16[2304,384]{0,1:T(8,128)(2,1)} %copy-done.8, bf16[2304,384]{0,1:T(8,128)(2,1)} %copy-done.7), kind=kOutput, calls=%fused_computation.2 | convolution fusion | flops 7259553792 | bytes 16121856 | tf_op jit(solution)/shard_map/dot_general | solution.py:27
  477.1 22.2 %all-to-all-done.2 = bf16[4,1,384,512]{3,2,1,0:T(8,128)(2,1)S(1)} async-done(((bf16[4,1,384,512]{3,2,1,0:T(8,128)(2,1)}), bf16[4,1,384,512]{3,2,1,0:T(8,128)(2,1)S(1)}, u32[]{:S(2)}, u32[]{:S(2)}) %all-to-all-start.2) | async-done | bytes 1572896 | tf_op jit(solution)/shard_map/all_to_all | solution.py:115
  499.3 7.5 %all-to-all-start.1 = ((bf16[32,72,2048]{2,1,0:T(8,128)(2,1)}), bf16[32,72,2048]{2,1,0:T(8,128)(2,1)}, u32[]{:S(2)}, u32[]{:S(2)}) async-start(bf16[32,72,2048]{2,1,0:T(8,128)(2,1)} %bitcast.75), calls=%async_computation.1 | async-start | bytes 18874368 | tf_op jit(solution)/shard_map/all_to_all | solution.py:86
  506.8 0.3 all-gather.2.cloned.1.call-start
  507.1 3.5 reduce-scatter.3.cloned.1.call-done
  510.6 4.9 subtract_convert_fusion
  515.5 0.0 all-gather.2.cloned.1.call-update
  515.5 1.6 copy.47
  517.1 2.6 copy.48
  519.7 132.3 %all-to-all-done.1 = bf16[32,72,2048]{2,1,0:T(8,128)(2,1)} async-done(((bf16[32,72,2048]{2,1,0:T(8,128)(2,1)}), bf16[32,72,2048]{2,1,0:T(8,128)(2,1)}, u32[]{:S(2)}, u32[]{:S(2)}) %all-to-all-start.1) | async-done | bytes 9437216 | tf_op jit(solution)/shard_map/all_to_all | solution.py:86
  652.0 13.7 %gather_fusion = bf16[1024,2048]{1,0:T(8,128)(2,1)} fusion(bf16[2304,2048]{1,0:T(8,128)(2,1)} %bitcast.13, s32[1024]{0:T(1024)S(1)} %broadcast_clamp_fusion), kind=kCustom, calls=%fused_computation | custom fusion | bytes 8392704 | tf_op jit(solution)/shard_map/gather | solution.py:95
  665.7 5.9 bitcast_reduce_fusion
  671.7 3.8 copy.53
  675.4 0.0 copy-done.1
  (8 shorter events, 0.1 us)
Async XLA Ops:
  7.2 13.5 %copy-start = (bf16[128,2048]{1,0:T(8,128)(2,1)S(1)}, bf16[128,2048]{1,0:T(8,128)(2,1)}, u32[]{:S(2)}) copy-start(bf16[128,2048]{1,0:T(8,128)(2,1)} %param.10) | copy-start | bytes 1572868
  7.2 449.6 %reduce-scatter.5.cloned.1.call-start = ((), (), s32[]{:S(2)}) async-start(), calls=%async_computation.7 | async-start | bytes 1966080 | tf_op jit(solution)/shard_map/reduce_scatter | solution.py:102
  398.6 9.5 %copy-start.4 = (bf16[1,2048,768]{2,1,0:T(8,128)(2,1)S(1)}, bf16[1,2048,768]{2,1,0:T(8,128)(2,1)}, u32[]{:S(2)}) copy-start(bf16[1,2048,768]{2,1,0:T(8,128)(2,1)} %param.14) | copy-start | bytes 9437188
  418.2 2.9 copy-start.6
  421.1 9.1 %copy-start.5 = (bf16[1,384,2048]{2,1,0:T(8,128)(2,1)S(1)}, bf16[1,384,2048]{2,1,0:T(8,128)(2,1)}, u32[]{:S(2)}) copy-start(bf16[1,384,2048]{2,1,0:T(8,128)(2,1)} %param.15) | copy-start | bytes 4718596
  430.0 80.6 %reduce-scatter.3.cloned.1.call-start = ((), (), s32[]{:S(2)}) async-start(), calls=%async_computation.5 | async-start | bytes 3932160 | tf_op jit(solution)/shard_map/reduce_scatter | solution.py:99
  438.8 1.2 copy-start.7
  438.8 1.8 copy-start.8
  451.9 4.9 copy-start.2
  451.9 4.9 copy-start.3
  460.9 38.4 %all-to-all-start.2 = ((bf16[4,1,384,512]{3,2,1,0:T(8,128)(2,1)}), bf16[4,1,384,512]{3,2,1,0:T(8,128)(2,1)S(1)}, u32[]{:S(2)}, u32[]{:S(2)}) async-start(bf16[4,1,384,512]{3,2,1,0:T(8,128)(2,1)} %stack.5), calls=%async_computation.4 | async-start | bytes 3145728 | tf_op jit(solution)/shard_map/all_to_all | solution.py:115
  499.3 152.7 %all-to-all-start.1 = ((bf16[32,72,2048]{2,1,0:T(8,128)(2,1)}), bf16[32,72,2048]{2,1,0:T(8,128)(2,1)}, u32[]{:S(2)}, u32[]{:S(2)}) async-start(bf16[32,72,2048]{2,1,0:T(8,128)(2,1)} %bitcast.75), calls=%async_computation.1 | async-start | bytes 18874368 | tf_op jit(solution)/shard_map/all_to_all | solution.py:86
  506.8 164.9 %all-gather.2.cloned.1.call-start = ((), (), s32[]{:S(2)}) async-start(), calls=%async_computation.6 | async-start | bytes 3932160 | tf_op jit(solution)/shard_map/all_gather | solution.py:118
  665.7 9.7 %copy-start.1 = (bf16[128,2048]{1,0:T(8,128)(2,1)S(1)}, bf16[128,2048]{1,0:T(8,128)(2,1)}, u32[]{:S(2)}) copy-start(bf16[128,2048]{1,0:T(8,128)(2,1)} %param.10) | copy-start | bytes 1572868
Sparse Core Ops, SparseCore 0:
  430.1 26.6 reduce-scatter.4
  459.8 50.7 reduce-scatter.2
  515.6 39.2 all-gather.1
